TPU v7x, 256 devices: a whole 4x4x8 slice. The times are simulated.
256 devices in a mesh: dp: 32 (over x, z_hi, core), expert: 8 (over z_lo, y).
Axes of the slice: x: 4, y: 4, z: 8 (z_hi: 4, z_lo: 2; z = z_hi * 2 + z_lo), core: 2. Of those that a mesh axis runs over, the one named last changes fastest.
Arguments:
- tokens: bfloat16 [65536, 2560], P(('dp', 'expert')), may hold values from -24 to 24
- routes: int32 [65536, 1], P(('dp', 'expert')), may hold values from 0 to 7; in each aligned block of 256 rows (0 to 255, 256 to 511, ...) at most 40 rows name the same one
- gate_levels: int32 [65536, 1], P(('dp', 'expert')), may hold values from 1 to 64
- w_gate: bfloat16 [8, 2560, 768], P('expert', 'dp'), may hold values from -0.125 to 0.125
- w_up: bfloat16 [8, 2560, 768], P('expert', 'dp'), may hold values from -0.125 to 0.125
- w_down: bfloat16 [8, 2560, 768], P('expert', 'dp'), may hold values from -0.21875 to 0.21875
- grad_out: bfloat16 [65536, 2560], P(('dp', 'expert')), may hold values from -24 to 24
Outputs:
- moe_out: bfloat16 [65536, 2560], P(('dp', 'expert'))
- grad_tokens: bfloat16 [65536, 2560], P(('dp', 'expert'))
- grad_gate: float32 [8, 2560, 768], P('expert', 'dp')
- grad_up: float32 [8, 2560, 768], P('expert', 'dp')
- grad_down: float32 [8, 2560, 768], P('expert', 'dp')
Inputs may be any that keep to these rules, and one draw needn't show every extreme that they name: `routes`: among the rows of one device, no expert is named by more than 40 tokens, a bound that some block reaches.
All inputs are finite; a program needn't handle non-finite values.
Results may differ from a plain program's by a relative error of at most 0.019.
Values may be sent and summed in bfloat16 or wider, within the bound.
No kernel may reach another device: no remote copies, remote signals or barrier semaphores. Data moves between devices by JAX's collectives and lax.ppermute only.
A program may use at most 128 MiB of HBM per device.

v0:
```python
import jax
import jax.numpy as jnp
from jax import lax
from jax.sharding import Mesh
from jax.sharding import PartitionSpec as P

TOP = 1
CHIPS = ("x", "zh")
DP = ("x", "zh", "core")


def contract_last(matrix_a, matrix_b):
    return lax.dot_general(
        matrix_a, matrix_b, (((1,), (1,)), ((), ())), preferred_element_type=jnp.float32
    )


def contract_first(matrix_a, matrix_b):
    return lax.dot_general(
        matrix_a, matrix_b, (((0,), (0,)), ((), ())), preferred_element_type=jnp.float32
    )


def swap_cores(value):
    return lax.ppermute(value, "core", perm=[(0, 1), (1, 0)])


def gather_weight(weight):
    own = lax.all_to_all(weight, "core", split_axis=1, concat_axis=0, tiled=True)
    own = lax.all_gather(own, CHIPS, axis=0, tiled=True)
    other = swap_cores(own)
    return jnp.concatenate([own, other], axis=1)


def scatter_grad(part):
    half = part.shape[1] // 2
    rounded = part.astype(jnp.bfloat16)
    arrived = swap_cores(rounded[:, half:])
    pair_sum = (rounded[:, :half].astype(jnp.float32) + arrived.astype(jnp.float32)).astype(
        jnp.bfloat16
    )
    chip_sum = lax.psum_scatter(pair_sum, CHIPS, scatter_dimension=0, tiled=True)
    block = lax.all_to_all(chip_sum, "core", split_axis=0, concat_axis=1, tiled=True)
    return block.astype(jnp.float32)


def shards(tokens, routes, gate_levels, w_gate, w_up, w_down, grad_out):
    experts = lax.axis_size("expert")
    tok_rows = tokens.shape[0]
    model_width = tokens.shape[1]
    capacity = min(tok_rows, tok_rows * TOP * 5 // (4 * experts))
    slot_count = experts * capacity
    expert_of = routes[:, 0]
    onehot = (expert_of[:, None] == jnp.arange(experts, dtype=jnp.int32)[None, :]).astype(jnp.int32)
    earlier = jnp.cumsum(onehot, axis=0) - onehot
    slot_rank = jnp.sum(earlier * onehot, axis=1)
    slot_index = expert_of * capacity + slot_rank
    source_row = (
        jnp.zeros((slot_count,), jnp.int32)
        .at[slot_index]
        .set(jnp.arange(tok_rows, dtype=jnp.int32))
    )
    filled = (
        jnp.zeros((slot_count, 1), jnp.bfloat16)
        .at[slot_index, 0]
        .set(jnp.ones((tok_rows,), jnp.bfloat16))
    )
    gate_weight = gate_levels.astype(jnp.float32) / 64.0

    def pack_rows(values):
        return (jnp.take(values, source_row, axis=0) * filled).reshape(
            experts, capacity, model_width
        )

    gate_full = gather_weight(w_gate[0])
    up_full = gather_weight(w_up[0])
    down_full = gather_weight(w_down[0])
    received = lax.all_to_all(
        pack_rows(tokens), "expert", split_axis=0, concat_axis=0, tiled=True
    ).reshape(slot_count, model_width)
    act_gate = jnp.dot(received, gate_full, preferred_element_type=jnp.float32)
    act_up = jnp.dot(received, up_full, preferred_element_type=jnp.float32)
    sigmoid_gate = jax.nn.sigmoid(act_gate)
    silu_gate = act_gate * sigmoid_gate
    hidden = (silu_gate * act_up).astype(jnp.bfloat16)
    expert_out = (
        contract_last(hidden, down_full)
        .astype(jnp.bfloat16)
        .reshape(experts, capacity, model_width)
    )
    returned = lax.all_to_all(
        expert_out, "expert", split_axis=0, concat_axis=0, tiled=True
    ).reshape(slot_count, model_width)
    moe_out = (gate_weight * jnp.take(returned, slot_index, axis=0).astype(jnp.float32)).astype(
        jnp.bfloat16
    )
    out_grad = (gate_weight * grad_out.astype(jnp.float32)).astype(jnp.bfloat16)
    grad_rows = lax.all_to_all(
        pack_rows(out_grad), "expert", split_axis=0, concat_axis=0, tiled=True
    ).reshape(slot_count, model_width)
    hidden_grad = jnp.dot(grad_rows, down_full, preferred_element_type=jnp.float32)
    gate_delta = (
        hidden_grad * act_up * sigmoid_gate * (1.0 + act_gate * (1.0 - sigmoid_gate))
    ).astype(jnp.bfloat16)
    up_delta = (hidden_grad * silu_gate).astype(jnp.bfloat16)
    token_grad = (contract_last(gate_delta, gate_full) + contract_last(up_delta, up_full)).astype(
        jnp.bfloat16
    )
    arrived = lax.all_to_all(
        token_grad.reshape(experts, capacity, model_width),
        "expert",
        split_axis=0,
        concat_axis=0,
        tiled=True,
    )
    grad_tokens = jnp.take(arrived.reshape(slot_count, model_width), slot_index, axis=0)
    grad_down = scatter_grad(contract_first(grad_rows, hidden))
    grad_gate = scatter_grad(contract_first(received, gate_delta))
    grad_up = scatter_grad(contract_first(received, up_delta))
    return (moe_out, grad_tokens, grad_gate[None], grad_up[None], grad_down[None])


def solution(mesh):
    dp_size, expert_size = mesh.devices.shape
    chips = dp_size // 2
    x_size = 4 if chips % 4 == 0 else 1
    grid = mesh.devices.reshape(x_size, chips // x_size, 2, expert_size)
    fine = Mesh(grid, DP + ("expert",))
    rows = P(DP + ("expert",), None)
    weights = P("expert", DP, None)
    in_specs = (rows, rows, rows, weights, weights, weights, rows)
    out_specs = (rows, rows, weights, weights, weights)
    return jax.shard_map(shards, mesh=fine, in_specs=in_specs, out_specs=out_specs, check_vma=False)
```

profile of v0, /device:TPU:1, one launch (start us, length us, event | category | flops | bytes accessed | tf_op | source)
XLA Modules:
  0.0 517.0 jit_solution(15889433307063467944)
XLA Ops:
  8.3 7.4 %all_to_all.116 = bf16[80,2,384]{2,0,1:T(8,128)(2,1)} all-to-all(bf16[80,2,384]{2,0,1:T(8,128)(2,1)S(1)} %copy.26), channel_id=1, replica_groups=mesh['x'=4,'zh'=4,'core'=2,'expert'=8] {'core'}, dimensions={1} | all-to-all | bytes 245760 | tf_op jit(solution)/shard_map/all_to_all | solution.py:29
  16.8 4.5 all_to_all.117
  22.3 4.5 all_to_all.118
  43.0 4.3 all-to-all-start.5
  47.3 35.1 %all-gather.8.cloned.1.call-done = bf16[2560,384]{1,0:T(8,128)(2,1)} async-done(((bf16[160,384]{1,0:T(8,128)(2,1)}), bf16[2560,384]{1,0:T(8,128)(2,1)}) %all-gather.8.cloned.1.call-update) | async-done | bytes 1966096 | tf_op jit(solution)/shard_map/all_gather | solution.py:30
  82.9 4.4 all-to-all-start
  87.4 53.1 %all-gather.6.cloned.1.call-done = bf16[2560,384]{1,0:T(8,128)(2,1)} async-done(((bf16[160,384]{1,0:T(8,128)(2,1)}), bf16[2560,384]{1,0:T(8,128)(2,1)}) %all-gather.6.cloned.1.call-update) | async-done | bytes 1966096 | tf_op jit(solution)/shard_map/all_gather | solution.py:30
  142.9 56.5 %all-gather.4.cloned.1.call-done = bf16[2560,384]{1,0:T(8,128)(2,1)} async-done(((bf16[160,384]{1,0:T(8,128)(2,1)}), bf16[2560,384]{1,0:T(8,128)(2,1)}) %all-gather.4.cloned.1.call-update) | async-done | bytes 1966096 | tf_op jit(solution)/shard_map/all_gather | solution.py:30
  207.8 4.6 constant_dynamic-update-slice_fusion.2
  215.3 4.2 fusion.9
  221.4 4.4 multiply_convert_fusion.3
  225.9 4.0 convolution_convert_fusion.2
  247.1 4.8 convolution_convert_fusion.3
  251.9 4.7 all-to-all-start.4
  264.4 3.9 fusion.11
  271.0 15.7 %all-to-all-done.4 = bf16[8,40,2560]{2,1,0:T(8,128)(2,1)S(1)} async-done(((bf16[8,40,2560]{2,1,0:T(8,128)(2,1)}), bf16[8,40,2560]{2,1,0:T(8,128)(2,1)S(1)}, u32[]{:S(2)}, u32[]{:S(2)}) %all-to-all-start.4) | async-done | bytes 1638432 | tf_op jit(solution)/shard_map/all_to_all | solution.py:91
  290.6 4.0 add_convert_fusion
  297.1 14.6 %all-to-all-done.6 = bf16[8,40,2560]{2,1,0:T(8,128)(2,1)S(1)} async-done(((bf16[8,40,2560]{2,1,0:T(8,128)(2,1)}), bf16[8,40,2560]{2,1,0:T(8,128)(2,1)S(1)}, u32[]{:S(2)}, u32[]{:S(2)}) %all-to-all-start.6) | async-done | bytes 1638432 | tf_op jit(solution)/shard_map/all_to_all | solution.py:109
  316.4 7.0 %reduce-scatter.4.cloned.1.call-done = bf16[160,384]{1,0:T(8,128)(2,1)} async-done(((bf16[2560,384]{1,0:T(8,128)(2,1)}), bf16[160,384]{1,0:T(8,128)(2,1)}) %reduce-scatter.4.cloned.1.call-update) | async-done | bytes 122896 | tf_op jit(solution)/shard_map/reduce_scatter | solution.py:42
  323.4 6.3 %all_to_all.119 = bf16[2,80,384]{2,1,0:T(8,128)(2,1)S(1)} all-to-all(bf16[2,80,384]{2,1,0:T(8,128)(2,1)} %bitcast.63), channel_id=1, replica_groups=mesh['x'=4,'zh'=4,'core'=2,'expert'=8] {'core'}, dimensions={0} | all-to-all | bytes 245760 | tf_op jit(solution)/shard_map/all_to_all | solution.py:43
  330.7 82.8 %reduce-scatter.6.cloned.1.call-done = bf16[160,384]{1,0:T(8,128)(2,1)} async-done(((bf16[2560,384]{1,0:T(8,128)(2,1)}), bf16[160,384]{1,0:T(8,128)(2,1)}) %reduce-scatter.6.cloned.1.call-update) | async-done | bytes 122896 | tf_op jit(solution)/shard_map/reduce_scatter | solution.py:42
  413.5 6.6 %all_to_all.120 = bf16[2,80,384]{2,1,0:T(8,128)(2,1)S(1)} all-to-all(bf16[2,80,384]{2,1,0:T(8,128)(2,1)} %bitcast.64), channel_id=1, replica_groups=mesh['x'=4,'zh'=4,'core'=2,'expert'=8] {'core'}, dimensions={0} | all-to-all | bytes 245760 | tf_op jit(solution)/shard_map/all_to_all | solution.py:43
  421.1 81.1 %reduce-scatter.8.cloned.1.call-done = bf16[160,384]{1,0:T(8,128)(2,1)} async-done(((bf16[2560,384]{1,0:T(8,128)(2,1)}), bf16[160,384]{1,0:T(8,128)(2,1)}) %reduce-scatter.8.cloned.1.call-update) | async-done | bytes 122896 | tf_op jit(solution)/shard_map/reduce_scatter | solution.py:42
  502.3 6.9 %all_to_all.121 = bf16[2,80,384]{2,1,0:T(8,128)(2,1)S(1)} all-to-all(bf16[2,80,384]{2,1,0:T(8,128)(2,1)} %bitcast.65), channel_id=1, replica_groups=mesh['x'=4,'zh'=4,'core'=2,'expert'=8] {'core'}, dimensions={0} | all-to-all | bytes 245760 | tf_op jit(solution)/shard_map/all_to_all | solution.py:43
  (117 shorter events, 77.0 us)
Async XLA Ops:
  7.2 27.0 %copy-start = (bf16[256,2560]{1,0:T(8,128)(2,1)S(1)}, bf16[256,2560]{1,0:T(8,128)(2,1)}, u32[]{:S(2)}) copy-start(bf16[256,2560]{1,0:T(8,128)(2,1)} %param.11) | copy-start | bytes 3932164
  7.2 19.7 %copy-start.12 = (s32[256,1]{0,1:T(1,128)S(1)}, s32[256,1]{0,1:T(1,128)}, u32[]{:S(2)}) copy-start(s32[256,1]{0,1:T(1,128)} %param.12) | copy-start | bytes 3076
  7.2 22.1 %copy-start.13 = (s32[256,1]{0,1:T(1,128)S(1)}, s32[256,1]{0,1:T(1,128)}, u32[]{:S(2)}) copy-start(s32[256,1]{0,1:T(1,128)} %param.13) | copy-start | bytes 3076
  7.2 75.2 %all-gather.8.cloned.1.call-start = ((), (), s32[]{:S(2)}) async-start(), calls=%async_computation.15 | async-start | bytes 2088960 | tf_op jit(solution)/shard_map/all_gather | solution.py:30
  15.8 124.8 %all-gather.6.cloned.1.call-start = ((), (), s32[]{:S(2)}) async-start(), calls=%async_computation.14 | async-start | bytes 2088960 | tf_op jit(solution)/shard_map/all_gather | solution.py:30
  21.3 178.1 %all-gather.4.cloned.1.call-start = ((), (), s32[]{:S(2)}) async-start(), calls=%async_computation.13 | async-start | bytes 2088960 | tf_op jit(solution)/shard_map/all_gather | solution.py:30
  34.1 5.3 %copy-start.2 = (bf16[320,2560]{1,0:T(8,128)(2,1)S(1)}, bf16[320,2560]{1,0:T(8,128)(2,1)}, u32[]{:S(2)}) copy-start(bf16[320,2560]{1,0:T(8,128)(2,1)} %gather_fusion.2) | copy-start | bytes 4915204
  43.0 39.9 %all-to-all-start.5 = ((bf16[8,40,2560]{2,1,0:T(8,128)(2,1)}), bf16[8,40,2560]{2,1,0:T(8,128)(2,1)}, u32[]{:S(2)}, u32[]{:S(2)}) async-start(bf16[8,40,2560]{2,1,0:T(8,128)(2,1)} %bitcast.17), calls=%async_computation.5 | async-start | bytes 3276800 | tf_op jit(solution)/shard_map/all_to_all | solution.py:98
  82.4 119.3 %copy-start.5 = (bf16[2560,384]{1,0:T(8,128)(2,1)S(1)}, bf16[2560,384]{1,0:T(8,128)(2,1)}, u32[]{:S(2)}) copy-start(bf16[2560,384]{1,0:T(8,128)(2,1)} %all-gather.8.cloned.1.call-done) | copy-start | bytes 5898244
  82.4 123.4 %collective-permute-start.2 = (bf16[2560,384]{1,0:T(8,128)(2,1)}, bf16[2560,384]{1,0:T(8,128)(2,1)}, u32[]{:S(2)}, u32[]{:S(2)}) collective-permute-start(bf16[2560,384]{1,0:T(8,128)(2,1)} %all-gather.8.cloned.1.call-done), channel_id=1, source_target_pairs={{0,8},{8,0},{1,9},{9,1},{2,10},{10,2},{3,11},{11,3},{4,12},{12,4},... | collective-permute-start | bytes 5898248 | tf_op jit(solution)/shard_map/ppermute | solution.py:25
  82.9 132.3 %all-to-all-start = ((bf16[8,40,2560]{2,1,0:T(8,128)(2,1)}), bf16[8,40,2560]{2,1,0:T(8,128)(2,1)}, u32[]{:S(2)}, u32[]{:S(2)}) async-start(bf16[8,40,2560]{2,1,0:T(8,128)(2,1)} %bitcast.7), calls=%async_computation | async-start | bytes 3276800 | tf_op jit(solution)/shard_map/all_to_all | solution.py:78
  87.3 236.0 %reduce-scatter.4.cloned.1.call-start = ((), (), s32[]{:S(2)}) async-start(), calls=%async_computation.16 | async-start | bytes 2088960 | tf_op jit(solution)/shard_map/reduce_scatter | solution.py:42
  140.5 67.2 %collective-permute-start.1 = (bf16[2560,384]{1,0:T(8,128)(2,1)}, bf16[2560,384]{1,0:T(8,128)(2,1)}, u32[]{:S(2)}, u32[]{:S(2)}) collective-permute-start(bf16[2560,384]{1,0:T(8,128)(2,1)} %all-gather.6.cloned.1.call-done), channel_id=1, source_target_pairs={{0,8},{8,0},{1,9},{9,1},{2,10},{10,2},{3,11},{11,3},{4,12},{12,4},... | collective-permute-start | bytes 5898248 | tf_op jit(solution)/shard_map/ppermute | solution.py:25
  199.4 20.1 %collective-permute-start = (bf16[2560,384]{1,0:T(8,128)(2,1)}, bf16[2560,384]{1,0:T(8,128)(2,1)}, u32[]{:S(2)}, u32[]{:S(2)}) collective-permute-start(bf16[2560,384]{1,0:T(8,128)(2,1)} %all-gather.4.cloned.1.call-done), channel_id=1, source_target_pairs={{0,8},{8,0},{1,9},{9,1},{2,10},{10,2},{3,11},{11,3},{4,12},{12,4},... | collective-permute-start | bytes 5898248 | tf_op jit(solution)/shard_map/ppermute | solution.py:25
  225.8 21.3 %copy-start.16 = (bf16[320,768]{1,0:T(8,128)(2,1)}, bf16[320,768]{1,0:T(8,128)(2,1)S(1)}, u32[]{:S(2)}) copy-start(bf16[320,768]{1,0:T(8,128)(2,1)S(1)} %get-tuple-element.11) | copy-start | bytes 1474564
  230.1 5.0 collective-permute-start.3
  237.0 176.5 %reduce-scatter.6.cloned.1.call-start = ((), (), s32[]{:S(2)}) async-start(), calls=%async_computation.17 | async-start | bytes 2088960 | tf_op jit(solution)/shard_map/reduce_scatter | solution.py:42
  241.0 4.3 collective-permute-start.4
  251.9 4.7 copy-start.17
  251.9 34.7 %all-to-all-start.4 = ((bf16[8,40,2560]{2,1,0:T(8,128)(2,1)}), bf16[8,40,2560]{2,1,0:T(8,128)(2,1)S(1)}, u32[]{:S(2)}, u32[]{:S(2)}) async-start(bf16[8,40,2560]{2,1,0:T(8,128)(2,1)} %bitcast.15), calls=%async_computation.4 | async-start | bytes 3276800 | tf_op jit(solution)/shard_map/all_to_all | solution.py:91
  263.7 26.9 %collective-permute-start.5 = (bf16[2560,384]{1,0:T(8,128)(2,1)}, bf16[2560,384]{1,0:T(8,128)(2,1)}, u32[]{:S(2)}, u32[]{:S(2)}) collective-permute-start(bf16[2560,384]{1,0:T(8,128)(2,1)} %slice.48), channel_id=1, source_target_pairs={{0,8},{8,0},{1,9},{9,1},{2,10},{10,2},{3,11},{11,3},{4,12},{12,4},... | collective-permute-start | bytes 5898248 | tf_op jit(solution)/shard_map/ppermute | solution.py:25
  286.7 25.1 %all-to-all-start.6 = ((bf16[8,40,2560]{2,1,0:T(8,128)(2,1)}), bf16[8,40,2560]{2,1,0:T(8,128)(2,1)S(1)}, u32[]{:S(2)}, u32[]{:S(2)}) async-start(bf16[8,40,2560]{2,1,0:T(8,128)(2,1)} %bitcast.59), calls=%async_computation.6 | async-start | bytes 3276800 | tf_op jit(solution)/shard_map/all_to_all | solution.py:109
  290.6 211.7 %reduce-scatter.8.cloned.1.call-start = ((), (), s32[]{:S(2)}) async-start(), calls=%async_computation.18 | async-start | bytes 2088960 | tf_op jit(solution)/shard_map/reduce_scatter | solution.py:42
  329.6 180.5 %copy-start.1 = (bf16[256,2560]{1,0:T(8,128)(2,1)S(1)}, bf16[256,2560]{1,0:T(8,128)(2,1)}, u32[]{:S(2)}) copy-start(bf16[256,2560]{1,0:T(8,128)(2,1)} %param.11) | copy-start | bytes 3932164
  (10 other events, 35.0 us)
Sparse Core Ops, SparseCore 0:
  15.9 66.5 all-gather.7
  84.9 55.5 all-gather.5
  143.0 56.3 all-gather.3
  237.2 86.1 reduce-scatter.3
  327.2 86.2 reduce-scatter.5
  416.9 85.3 reduce-scatter.7
where the time goes:
time: 518 us; the launch traced here: 517 us
  waiting for transfers between devices  353 us (68%)
  local copies, waits for them, and re-layouts  36.8 us (7%)
  blocking collectives  36.2 us (7%)
  matrix products  34.2 us (7%)
  starting transfers between devices  25.6 us (5%)
  other arithmetic  16.4 us (3%)
  between operations  14.6 us (3%)
    reduce_scatter x3, waiting for transfers between devices, scatter_grad(): lax.psum_scatter(pair_sum, CHIPS, scatter_dimension=0, tiled=True)  171 us
    all_gather x3, waiting for transfers between devices, gather_weight(): own = lax.all_gather(own, CHIPS, axis=0, tiled=True)  145 us
    all_to_all x3, blocking collectives, scatter_grad(): lax.all_to_all(chip_sum, 'core', split_axis=0, concat_axis=1, tiled=True)  19.7 us
    all_to_all x3, blocking collectives, gather_weight(): lax.all_to_all(weight, 'core', split_axis=1, concat_axis=0, tiled=True)  16.5 us
    all_to_all x1, waiting for transfers between devices, shards(): lax.all_to_all(expert_out, 'expert', split_axis=0, concat_axis=0, tiled=T...  15.7 us
    all_to_all x1, waiting for transfers between devices, shards(): lax.all_to_all(token_grad.reshape(experts, capacity, model_width), 'exper...  14.6 us
    dot_general x3, matrix products, contract_last(): lax.dot_general(matrix_a, matrix_b, (((1,), (1,)), ((), ())), preferred_e...  11.4 us
    dot_general x3, matrix products, contract_first(): lax.dot_general(matrix_a, matrix_b, (((0,), (0,)), ((), ())), preferred_e...  11.4 us
  transfers between devices with their start and end apart: 16, of which 10 were waited for; matrix products, arithmetic and copies ran while one was open for 13% of the time, Pallas kernels for 0%

commit v1 on v0

--- a/solution.py
+++ b/solution.py
@@ -26,8 +26,15 @@
 
 
 def gather_weight(weight):
+
+    def squares_follow(row_axis, arr_in):
+        newest = lax.all_to_all(
+            jnp.stack(lax.axis_size(row_axis) * [arr_in], axis=0), row_axis, 0, 0
+        )
+        return jnp.concatenate(newest, axis=0)
+
     own = lax.all_to_all(weight, "core", split_axis=1, concat_axis=0, tiled=True)
-    own = lax.all_gather(own, CHIPS, axis=0, tiled=True)
+    own = squares_follow(CHIPS, own)
     other = swap_cores(own)
     return jnp.concatenate([own, other], axis=1)
 

time: 518 us -> 569 us (1.098)
  blocking collectives: 36.2 us -> 232 us
  waiting for transfers between devices: 353 us -> 217 us
  local copies, waits for them, and re-layouts: 36.8 us -> 28.3 us
    all_to_all x0 -> x4, blocking collectives: none -> 204 us  [the longest x3 179 us: squares_follow(): lax.all_to_all(jnp.stack(lax.axis_size(row_axis) * [arr_in], axis=0), row...]
    all_gather x3 -> x0, waiting for transfers between devices: 145 us -> none  [gather_weight(): own = lax.all_gather(own, CHIPS, axis=0, tiled=True)]
    all_to_all x1, waiting for transfers between devices: 0.01 us -> 8.5 us  [shards(): lax.all_to_all(pack_rows(tokens), 'expert', split_axis=0, concat_axis=0,...]
    concatenate x3 -> x0, local copies, waits for them, and re-layouts: 8.47 us -> none  [gather_weight(): return jnp.concatenate([own, other], axis=1)]
    all_to_all x3 -> x2, blocking collectives: 16.5 us -> 8.3 us  [gather_weight(): lax.all_to_all(weight, 'core', split_axis=1, concat_axis=0, tiled=True)]
  transfers between devices with their start and end apart: 16 -> 13, of which waited for: 10 -> 9; matrix products, arithmetic and copies ran while one was open for 13% -> 11% of each run, Pallas kernels for 0% -> 0%
where the time goes in v1:
time: 569 us; the launch traced here: 567 us
  blocking collectives  232 us (41%)
  waiting for transfers between devices  217 us (38%)
  matrix products  33.6 us (6%)
  local copies, waits for them, and re-layouts  28.3 us (5%)
  starting transfers between devices  23.7 us (4%)
  other arithmetic  18.5 us (3%)
  between operations  14.1 us (2%)
    all_to_all x3, blocking collectives, squares_follow(): lax.all_to_all(jnp.stack(lax.axis_size(row_axis) * [arr_in], axis=0), row...  179 us
    reduce_scatter x3, waiting for transfers between devices, scatter_grad(): lax.psum_scatter(pair_sum, CHIPS, scatter_dimension=0, tiled=True)  168 us
    all_to_all x1, blocking collectives, shards(): lax.all_to_all(pack_rows(out_grad), 'expert', split_axis=0, concat_axis=0...  25.1 us
    all_to_all x3, blocking collectives, scatter_grad(): lax.all_to_all(chip_sum, 'core', split_axis=0, concat_axis=1, tiled=True)  19.8 us
    all_to_all x1, waiting for transfers between devices, shards(): lax.all_to_all(expert_out, 'expert', split_axis=0, concat_axis=0, tiled=T...  14.3 us
    all_to_all x1, waiting for transfers between devices, shards(): lax.all_to_all(token_grad.reshape(experts, capacity, model_width), 'exper...  13.7 us
    ppermute x6, waiting for transfers between devices, swap_cores(): return lax.ppermute(value, 'core', perm=[(0, 1), (1, 0)])  12.3 us
    dot_general x3, matrix products, contract_last(): lax.dot_general(matrix_a, matrix_b, (((1,), (1,)), ((), ())), preferred_e...  11.6 us
  transfers between devices with their start and end apart: 13, of which 9 were waited for; matrix products, arithmetic and copies ran while one was open for 11% of the time, Pallas kernels for 0%

profile of v1, /device:TPU:1, one launch (start us, length us, event | category | flops | bytes accessed | tf_op | source)
XLA Modules:
  0.0 567.3 jit_solution(12946420057708611513)
XLA Ops:
  8.9 6.6 %all-to-all-start.5 = ((bf16[80,2,384]{2,0,1:T(8,128)(2,1)}), bf16[80,2,384]{2,0,1:T(8,128)(2,1)S(1)}, u32[]{:S(2)}, u32[]{:S(2)}) async-start(bf16[80,2,384]{2,0,1:T(8,128)(2,1)} %copy.26), calls=%async_computation.5 | async-start | bytes 245760 | tf_op jit(solution)/shard_map/all_to_all | solution.py:36
  38.0 4.8 all_to_all.123
  42.8 25.1 %all_to_all.124 = bf16[8,40,2560]{2,1,0:T(8,128)(2,1)} all-to-all(bf16[8,40,2560]{2,1,0:T(8,128)(2,1)S(1)} %bitcast.56), channel_id=1, replica_groups=mesh['x'=4,'zh'=4,'core'=2,'expert'=8] {'expert'}, dimensions={0} | all-to-all | bytes 3276800 | tf_op jit(solution)/shard_map/all_to_all | solution.py:105
  68.1 57.5 %all_to_all.125 = bf16[16,160,384]{2,1,0:T(8,128)(2,1)} all-to-all(bf16[16,160,384]{2,1,0:T(8,128)(2,1)S(1)} %stack.17), channel_id=1, replica_groups=mesh['x'=4,'zh'=4,'core'=2,'expert'=8] {'x','zh'}, dimensions={0} | all-to-all | bytes 3932160 | tf_op jit(solution)/shard_map/all_to_all | solution.py:31
  125.8 76.9 %all_to_all.126 = bf16[16,160,384]{2,1,0:T(8,128)(2,1)S(1)} all-to-all(bf16[16,160,384]{2,1,0:T(8,128)(2,1)S(1)} %stack.15), channel_id=1, replica_groups=mesh['x'=4,'zh'=4,'core'=2,'expert'=8] {'x','zh'}, dimensions={0} | all-to-all | bytes 3932160 | tf_op jit(solution)/shard_map/all_to_all | solution.py:31
  202.9 44.3 %all_to_all.127 = bf16[16,160,384]{2,1,0:T(8,128)(2,1)} all-to-all(bf16[16,160,384]{2,1,0:T(8,128)(2,1)S(1)} %stack.13), channel_id=1, replica_groups=mesh['x'=4,'zh'=4,'core'=2,'expert'=8] {'x','zh'}, dimensions={0} | all-to-all | bytes 3932160 | tf_op jit(solution)/shard_map/all_to_all | solution.py:31
  247.2 4.3 all-to-all-start
  254.3 5.1 collective-permute-done.2
  264.2 8.5 %all-to-all-done = bf16[8,40,2560]{2,1,0:T(8,128)(2,1)} async-done(((bf16[8,40,2560]{2,1,0:T(8,128)(2,1)}), bf16[8,40,2560]{2,1,0:T(8,128)(2,1)}, u32[]{:S(2)}, u32[]{:S(2)}) %all-to-all-start) | async-done | bytes 1638432 | tf_op jit(solution)/shard_map/all_to_all | solution.py:85
  276.3 3.8 multiply_convert_fusion.3
  280.2 4.2 convolution_convert_fusion.2
  302.4 4.2 convolution_convert_fusion.3
  306.6 3.9 all-to-all-start.7
  321.1 4.4 fusion
  325.5 14.3 %all-to-all-done.7 = bf16[8,40,2560]{2,1,0:T(8,128)(2,1)S(1)} async-done(((bf16[8,40,2560]{2,1,0:T(8,128)(2,1)}), bf16[8,40,2560]{2,1,0:T(8,128)(2,1)S(1)}, u32[]{:S(2)}, u32[]{:S(2)}) %all-to-all-start.7) | async-done | bytes 1638432 | tf_op jit(solution)/shard_map/all_to_all | solution.py:98
  339.8 4.2 all-to-all-start.9
  344.0 4.0 add_convert_fusion
  351.2 13.7 %all-to-all-done.9 = bf16[8,40,2560]{2,1,0:T(8,128)(2,1)S(1)} async-done(((bf16[8,40,2560]{2,1,0:T(8,128)(2,1)}), bf16[8,40,2560]{2,1,0:T(8,128)(2,1)S(1)}, u32[]{:S(2)}, u32[]{:S(2)}) %all-to-all-start.9) | async-done | bytes 1638432 | tf_op jit(solution)/shard_map/all_to_all | solution.py:116
  369.6 3.8 reduce-scatter.4.cloned.1.call-done
  373.4 6.6 %all_to_all.128 = bf16[2,80,384]{2,1,0:T(8,128)(2,1)S(1)} all-to-all(bf16[2,80,384]{2,1,0:T(8,128)(2,1)} %bitcast.73), channel_id=1, replica_groups=mesh['x'=4,'zh'=4,'core'=2,'expert'=8] {'core'}, dimensions={0} | all-to-all | bytes 245760 | tf_op jit(solution)/shard_map/all_to_all | solution.py:50
  381.0 82.6 %reduce-scatter.6.cloned.1.call-done = bf16[160,384]{1,0:T(8,128)(2,1)} async-done(((bf16[2560,384]{1,0:T(8,128)(2,1)}), bf16[160,384]{1,0:T(8,128)(2,1)}) %reduce-scatter.6.cloned.1.call-update) | async-done | bytes 122896 | tf_op jit(solution)/shard_map/reduce_scatter | solution.py:49
  463.6 6.6 %all_to_all.129 = bf16[2,80,384]{2,1,0:T(8,128)(2,1)S(1)} all-to-all(bf16[2,80,384]{2,1,0:T(8,128)(2,1)} %bitcast.74), channel_id=1, replica_groups=mesh['x'=4,'zh'=4,'core'=2,'expert'=8] {'core'}, dimensions={0} | all-to-all | bytes 245760 | tf_op jit(solution)/shard_map/all_to_all | solution.py:50
  471.3 81.9 %reduce-scatter.8.cloned.1.call-done = bf16[160,384]{1,0:T(8,128)(2,1)} async-done(((bf16[2560,384]{1,0:T(8,128)(2,1)}), bf16[160,384]{1,0:T(8,128)(2,1)}) %reduce-scatter.8.cloned.1.call-update) | async-done | bytes 122896 | tf_op jit(solution)/shard_map/reduce_scatter | solution.py:49
  553.1 6.6 %all_to_all.130 = bf16[2,80,384]{2,1,0:T(8,128)(2,1)S(1)} all-to-all(bf16[2,80,384]{2,1,0:T(8,128)(2,1)} %bitcast.75), channel_id=1, replica_groups=mesh['x'=4,'zh'=4,'core'=2,'expert'=8] {'core'}, dimensions={0} | all-to-all | bytes 245760 | tf_op jit(solution)/shard_map/all_to_all | solution.py:50
  (112 shorter events, 75.3 us)
Async XLA Ops:
  7.2 18.2 %copy-start = (bf16[256,2560]{1,0:T(8,128)(2,1)S(1)}, bf16[256,2560]{1,0:T(8,128)(2,1)}, u32[]{:S(2)}) copy-start(bf16[256,2560]{1,0:T(8,128)(2,1)} %param.11) | copy-start | bytes 3932164
  8.9 25.6 %all-to-all-start.5 = ((bf16[80,2,384]{2,0,1:T(8,128)(2,1)}), bf16[80,2,384]{2,0,1:T(8,128)(2,1)S(1)}, u32[]{:S(2)}, u32[]{:S(2)}) async-start(bf16[80,2,384]{2,0,1:T(8,128)(2,1)} %copy.26), calls=%async_computation.5 | async-start | bytes 245760 | tf_op jit(solution)/shard_map/all_to_all | solution.py:36
  25.3 6.1 %copy-start.2 = (bf16[320,2560]{1,0:T(8,128)(2,1)S(1)}, bf16[320,2560]{1,0:T(8,128)(2,1)}, u32[]{:S(2)}) copy-start(bf16[320,2560]{1,0:T(8,128)(2,1)} %gather_fusion.2) | copy-start | bytes 4915204
  202.7 70.0 %copy-start.5 = (bf16[16,160,384]{2,1,0:T(8,128)(2,1)}, bf16[16,160,384]{2,1,0:T(8,128)(2,1)S(1)}, u32[]{:S(2)}) copy-start(bf16[16,160,384]{2,1,0:T(8,128)(2,1)S(1)} %all_to_all.126) | copy-start | bytes 5898244
  247.2 25.5 %all-to-all-start = ((bf16[8,40,2560]{2,1,0:T(8,128)(2,1)}), bf16[8,40,2560]{2,1,0:T(8,128)(2,1)}, u32[]{:S(2)}, u32[]{:S(2)}) async-start(bf16[8,40,2560]{2,1,0:T(8,128)(2,1)} %bitcast.7), calls=%async_computation | async-start | bytes 3276800 | tf_op jit(solution)/shard_map/all_to_all | solution.py:85
  251.5 121.9 %reduce-scatter.4.cloned.1.call-start = ((), (), s32[]{:S(2)}) async-start(), calls=%async_computation.16 | async-start | bytes 2088960 | tf_op jit(solution)/shard_map/reduce_scatter | solution.py:49
  251.5 7.9 %collective-permute-start.2 = (bf16[2560,384]{1,0:T(8,128)(2,1)}, bf16[2560,384]{1,0:T(8,128)(2,1)S(1)}, u32[]{:S(2)}, u32[]{:S(2)}) collective-permute-start(bf16[2560,384]{1,0:T(8,128)(2,1)} %bitcast.63), channel_id=1, source_target_pairs={{0,8},{8,0},{1,9},{9,1},{2,10},{10,2},{3,11},{11,3},{4,12},{12,4},... | collective-permute-start | bytes 5898248 | tf_op jit(solution)/shard_map/ppermute | solution.py:25
  253.8 18.9 %collective-permute-start.1 = (bf16[2560,384]{1,0:T(8,128)(2,1)S(1)}, bf16[2560,384]{1,0:T(8,128)(2,1)}, u32[]{:S(2)}, u32[]{:S(2)}) collective-permute-start(bf16[2560,384]{1,0:T(8,128)(2,1)S(1)} %bitcast.57), channel_id=1, source_target_pairs={{0,8},{8,0},{1,9},{9,1},{2,10},{10,2},{3,11},{11,3},{4,12},{12,4},... | collective-permute-start | bytes 5898248 | tf_op jit(solution)/shard_map/ppermute | solution.py:25
  253.9 22.4 %collective-permute-start = (bf16[2560,384]{1,0:T(8,128)(2,1)}, bf16[2560,384]{1,0:T(8,128)(2,1)}, u32[]{:S(2)}, u32[]{:S(2)}) collective-permute-start(bf16[2560,384]{1,0:T(8,128)(2,1)} %bitcast.60), channel_id=1, source_target_pairs={{0,8},{8,0},{1,9},{9,1},{2,10},{10,2},{3,11},{11,3},{4,12},{12,4},... | collective-permute-start | bytes 5898248 | tf_op jit(solution)/shard_map/ppermute | solution.py:25
  272.7 3.6 copy-start.7
  280.1 4.2 copy-start.15
  280.1 10.9 %copy-start.17 = (bf16[320,768]{1,0:T(8,128)(2,1)}, bf16[320,768]{1,0:T(8,128)(2,1)S(1)}, u32[]{:S(2)}) copy-start(bf16[320,768]{1,0:T(8,128)(2,1)S(1)} %get-tuple-element.10) | copy-start | bytes 1474564
  280.1 20.7 %copy-start.19 = (bf16[320,768]{1,0:T(8,128)(2,1)}, bf16[320,768]{1,0:T(8,128)(2,1)S(1)}, u32[]{:S(2)}) copy-start(bf16[320,768]{1,0:T(8,128)(2,1)S(1)} %get-tuple-element.11) | copy-start | bytes 1474564
  284.6 4.6 collective-permute-start.3
  291.0 172.6 %reduce-scatter.6.cloned.1.call-start = ((), (), s32[]{:S(2)}) async-start(), calls=%async_computation.17 | async-start | bytes 2088960 | tf_op jit(solution)/shard_map/reduce_scatter | solution.py:49
  295.0 4.1 collective-permute-start.4
  306.6 4.0 copy-start.10
  306.6 33.2 %all-to-all-start.7 = ((bf16[8,40,2560]{2,1,0:T(8,128)(2,1)}), bf16[8,40,2560]{2,1,0:T(8,128)(2,1)S(1)}, u32[]{:S(2)}, u32[]{:S(2)}) async-start(bf16[8,40,2560]{2,1,0:T(8,128)(2,1)} %bitcast.69), calls=%async_computation.7 | async-start | bytes 3276800 | tf_op jit(solution)/shard_map/all_to_all | solution.py:98
  317.2 3.9 copy-start.8
  317.2 3.9 copy-start.16
  317.2 26.8 %collective-permute-start.5 = (bf16[2560,384]{1,0:T(8,128)(2,1)}, bf16[2560,384]{1,0:T(8,128)(2,1)}, u32[]{:S(2)}, u32[]{:S(2)}) collective-permute-start(bf16[2560,384]{1,0:T(8,128)(2,1)} %slice.48), channel_id=1, source_target_pairs={{0,8},{8,0},{1,9},{9,1},{2,10},{10,2},{3,11},{11,3},{4,12},{12,4},... | collective-permute-start | bytes 5898248 | tf_op jit(solution)/shard_map/ppermute | solution.py:25
  339.8 25.1 %all-to-all-start.9 = ((bf16[8,40,2560]{2,1,0:T(8,128)(2,1)}), bf16[8,40,2560]{2,1,0:T(8,128)(2,1)S(1)}, u32[]{:S(2)}, u32[]{:S(2)}) async-start(bf16[8,40,2560]{2,1,0:T(8,128)(2,1)} %bitcast.68), calls=%async_computation.9 | async-start | bytes 3276800 | tf_op jit(solution)/shard_map/all_to_all | solution.py:116
  344.0 209.1 %reduce-scatter.8.cloned.1.call-start = ((), (), s32[]{:S(2)}) async-start(), calls=%async_computation.18 | async-start | bytes 2088960 | tf_op jit(solution)/shard_map/reduce_scatter | solution.py:49
  379.9 180.8 %copy-start.1 = (bf16[256,2560]{1,0:T(8,128)(2,1)S(1)}, bf16[256,2560]{1,0:T(8,128)(2,1)}, u32[]{:S(2)}) copy-start(bf16[256,2560]{1,0:T(8,128)(2,1)} %param.11) | copy-start | bytes 3932164
  (9 other events, 18.1 us)
Sparse Core Ops, SparseCore 0:
  291.1 82.1 reduce-scatter.3
  377.3 86.2 reduce-scatter.5
  467.1 85.9 reduce-scatter.7
